TPU v7x, 32 devices: a whole 2x2x4 slice. The times are simulated.
32 devices in a mesh: grp: 8 (over y, x, core), rep: 4 (over z).
Axes of the slice: x: 2, y: 2, z: 4, core: 2. Of those that a mesh axis runs over, the one named last changes fastest.
Arguments:
- features: bfloat16 [4096, 256], P(('grp', 'rep')), may hold values from -0.0625 to 0.0625
- weight: bfloat16 [256, 256], replicated, may hold values from -0.375 to 0.375
- preact: bfloat16 [4096, 256], P(('grp', 'rep')), may hold values from -6 to 6
- grad_out: bfloat16 [4096, 256], P(('grp', 'rep')), may hold values from -1.5 to 1.5
- degree: int32 [4096], P(('grp', 'rep')), may hold values from 1 to 64
- tile_values: bfloat16 [256, 4, 128, 128], P(('grp', 'rep')), may hold values from 0 to 1
- tile_rows: int32 [256, 4], P(('grp', 'rep')), may hold values from -1 to 3, as said below
Outputs:
- input_grad: float32 [4096, 256], P(('grp', 'rep'))
- weight_grad: float32 [256, 256], replicated
Inputs may be any that keep to these rules, and one draw needn't show every extreme that they name: `tile_rows`: each of the 8 rows of one device (aligned blocks) has up to 4 live slots; in every such block some row has all 4 slots live.
All inputs are finite; a program needn't handle non-finite values.
Results may differ from a plain program's by a relative error of at most 0.013.
Values may be sent and summed in bfloat16 or wider, within the bound.
No kernel may reach another device: no remote copies, remote signals or barrier semaphores. Data moves between devices by JAX's collectives and lax.ppermute only.
A program may use at most 128 MiB of HBM per device.

v0:
```python
import jax
import jax.numpy as jnp
from jax import lax
from jax.sharding import PartitionSpec as P

HIGHEST = lax.Precision.HIGHEST


def gather_rep(x):
    reps = lax.axis_size("rep")
    me = lax.axis_index("rep")
    parts = [x]
    for shift in range(1, reps):
        parts.append(lax.ppermute(x, "rep", [((i + shift) % reps, i) for i in range(reps)]))
    stacked = jnp.stack(parts)
    return jnp.roll(stacked, me, axis=0)


def all_reduce_a2a(w, axes):
    count = 1
    for name in axes:
        count *= lax.axis_size(name)
    chunks = w.reshape(count, -1)
    owned = lax.all_to_all(chunks, axes, 0, 0, tiled=True).reshape(count, -1).sum(0)
    spread = jnp.broadcast_to(owned[None], (count, owned.shape[0]))
    return lax.all_to_all(spread, axes, 0, 0, tiled=True).reshape(w.shape)


def per_device(features, weight, preact, grad_out, degree, tile_values, tile_rows):
    rows_here, width = features.shape
    col_tiles, slots, edge, _ = tile_values.shape
    reps = lax.axis_size("rep")
    row_tiles = reps * rows_here // edge
    inverse = lax.rsqrt(degree.astype(jnp.float32))[:, None]
    grad_pre = jnp.where(preact > 0, grad_out, jnp.zeros_like(grad_out))
    scaled = (features.astype(jnp.float32) * inverse).astype(jnp.bfloat16)
    projected = (
        lax.dot_general(
            grad_pre, weight, (((1,), (1,)), ((), ())), preferred_element_type=jnp.float32
        )
        * inverse
    ).astype(jnp.bfloat16)
    columns = lax.all_gather(scaled, "grp", axis=0, tiled=True).reshape(col_tiles, edge, width)
    degree_lanes = jnp.broadcast_to(degree.astype(jnp.bfloat16)[:, None], (rows_here, 128))
    packed = jnp.concatenate([projected, grad_pre, degree_lanes], axis=1)
    block = gather_rep(packed).reshape(reps * rows_here, -1)
    block_proj = block[:, :width].reshape(row_tiles, edge, width)
    block_grad = block[:, width : 2 * width].astype(jnp.float32)
    block_inverse = lax.rsqrt(block[:, 2 * width : 2 * width + 1].astype(jnp.float32))
    tile_live = tile_rows >= 0
    clipped = jnp.where(tile_live, tile_rows, 0)
    onehot = (
        (clipped[..., None] == jnp.arange(row_tiles, dtype=jnp.int32)) & tile_live[..., None]
    ).astype(jnp.float32)
    product = jnp.einsum("csij,cjf->csif", tile_values, columns, preferred_element_type=jnp.float32)
    partial = jnp.einsum("csh,csif->hif", onehot, product, precision=HIGHEST)
    partial = partial.reshape(row_tiles * edge, width) * block_inverse
    weight_local = lax.dot_general(
        partial,
        block_grad,
        (((0,), (0,)), ((), ())),
        precision=HIGHEST,
        preferred_element_type=jnp.float32,
    )
    picked = jnp.take(block_proj, clipped, axis=0)
    picked = jnp.where(tile_live[:, :, None, None], picked, jnp.zeros_like(picked))
    result = jnp.einsum("csij,csif->cjf", tile_values, picked, preferred_element_type=jnp.float32)
    terms = lax.all_to_all(result, "grp", 0, 0, tiled=True)
    input_grad = terms.sum(0) * inverse
    weight_grad = all_reduce_a2a(weight_local, ("grp", "rep"))
    return (input_grad, weight_grad)


def solution(mesh):
    return jax.shard_map(
        per_device,
        mesh=mesh,
        in_specs=(
            P(("grp", "rep"), None),
            P(),
            P(("grp", "rep"), None),
            P(("grp", "rep"), None),
            P(("grp", "rep")),
            P(("grp", "rep"), None, None, None),
            P(("grp", "rep"), None),
        ),
        out_specs=(P(("grp", "rep"), None), P()),
        check_vma=False,
    )
```

profile of v0, /device:TPU:0, one launch (start us, length us, event | category | flops | bytes accessed | tf_op | source)
XLA Modules:
  0.0 101.6 jit_solution(6074562311005059718)
XLA Ops:
  0.6 0.0 copy-start
  0.6 0.7 convert_rsqrt_fusion
  1.4 0.7 convert_element_type.22
  2.1 0.9 compare_select_fusion
  2.9 1.1 %fusion.8 = bf16[128,256]{1,0:T(8,128)(2,1)S(1)} fusion(bf16[128,256]{1,0:T(8,128)(2,1)S(1)} %compare_select_fusion, bf16[256,256]{1,0:T(8,128)(2,1)} %param.8, f32[128]{0:T(128)S(1)} %convert_rsqrt_fusion), kind=kOutput, calls=%fused_computation.10 | convolution fusion | flops 16842752 | bytes 262656 | tf_op jit(solution)/shard_map/dot_general | solution.py:38
  4.0 0.1 broadcast_in_dim.44
  4.2 5.1 %collective-permute-start = (bf16[128,640]{1,0:T(8,128)(2,1)S(1)}, bf16[128,640]{1,0:T(8,128)(2,1)S(1)}, u32[]{:S(2)}, u32[]{:S(2)}) collective-permute-start(bf16[128,640]{1,0:T(8,128)(2,1)S(1)} %pad_maximum_fusion), channel_id=1, source_target_pairs={{1,0},{2,1},{3,2},{0,3},{5,4},{6,5},{7,6},{4,7},{9,8},{10,9},{11,1... | collective-permute-start | bytes 491528 | tf_op jit(solution)/shard_map/ppermute | solution.py:14
  9.3 0.0 collective-permute-start.1
  9.3 1.0 collective-permute-start.2
  10.3 0.7 broadcast_select_fusion
  11.0 0.7 broadcast_compare_fusion
  11.7 0.1 copy.27
  11.7 0.1 reshape.47
  11.8 0.1 copy.26
  11.9 0.1 copy.25
  12.1 1.9 %collective-permute-done = bf16[128,640]{1,0:T(8,128)(2,1)S(1)} collective-permute-done((bf16[128,640]{1,0:T(8,128)(2,1)S(1)}, bf16[128,640]{1,0:T(8,128)(2,1)S(1)}, u32[]{:S(2)}, u32[]{:S(2)}) %collective-permute-start) | collective-permute-done | bytes 163872 | tf_op jit(solution)/shard_map/ppermute | solution.py:14
  13.9 9.2 %collective-permute-done.1 = bf16[128,640]{1,0:T(8,128)(2,1)S(1)} collective-permute-done((bf16[128,640]{1,0:T(8,128)(2,1)S(1)}, bf16[128,640]{1,0:T(8,128)(2,1)S(1)}, u32[]{:S(2)}, u32[]{:S(2)}) %collective-permute-start.1) | collective-permute-done | bytes 163872 | tf_op jit(solution)/shard_map/ppermute | solution.py:14
  23.2 0.0 collective-permute-done.2
  23.3 0.1 constant_dynamic-slice_fusion
  23.4 0.0 copy-start.1
  23.4 0.8 copy-done.1
  24.3 0.7 gather_fusion
  24.9 2.4 %copy.28 = bf16[8,4,128,256]{2,3,1,0:T(8,128)(2,1)} copy(bf16[8,4,128,256]{3,2,1,0:T(8,128)(2,1)S(1)} %bitcast.43) | data formatting | bytes 4194304 | tf_op jit(solution)/shard_map/jit(_take)/gather | solution.py:65
  27.3 0.0 copy-done
  27.3 3.3 %fusion.5 = f32[8,128,256]{1,2,0:T(8,128)} fusion(bf16[8,4,128,128]{3,2,1,0:T(8,128)(2,1)S(1)} %copy-done, bf16[8,4,128,256]{2,3,1,0:T(8,128)(2,1)} %copy.28, pred[8,4]{1,0:T(8,128)(4,1)S(1)} %copy.26, pred[8,4]{1,0:T(8,128)(4,1)S(1)} %copy.25), kind=kOutput, calls=%fused_computation.7 | convolution fusion | flops 270532608 | bytes 4194368 | tf_op jit(solution)/shard_map/csij,csif->cjf/dot_general | solution.py:67
  30.7 0.0 copy-start.2
  30.7 3.9 %all-to-all-start = ((f32[8,128,256]{1,2,0:T(8,128)}), f32[8,128,256]{1,2,0:T(8,128)S(1)}, u32[]{:S(2)}, u32[]{:S(2)}) async-start(f32[8,128,256]{1,2,0:T(8,128)} %fusion.5), calls=%async_computation | async-start | bytes 2097152 | tf_op jit(solution)/shard_map/all_to_all | solution.py:68
  34.6 0.0 copy-done.2
  34.6 0.0 copy-start.3
  34.6 0.2 rsqrt_reduce_fusion
  34.7 15.2 %all-to-all-done = f32[8,128,256]{1,2,0:T(8,128)S(1)} async-done(((f32[8,128,256]{1,2,0:T(8,128)}), f32[8,128,256]{1,2,0:T(8,128)S(1)}, u32[]{:S(2)}, u32[]{:S(2)}) %all-to-all-start) | async-done | bytes 1048608 | tf_op jit(solution)/shard_map/all_to_all | solution.py:68
  50.0 0.1 reduce_sum.18
  50.0 0.1 copy.29
  50.1 0.0 copy-done.3
  50.1 0.7 multiply_convert_fusion
  50.9 8.9 %all_gather.3 = bf16[1024,256]{1,0:T(8,128)(2,1)S(1)} all-gather(bf16[128,256]{1,0:T(8,128)(2,1)S(1)} %get-tuple-element.6), channel_id=1, replica_groups=mesh['grp'=8,'rep'=4] {'grp'}, dimensions={0}, use_global_device_ids=true | all-gather | bytes 589824 | tf_op jit(solution)/shard_map/all_gather | solution.py:43
  59.8 2.7 %convolution_bitcast_fusion = f32[8,4,128,256]{2,3,1,0:T(8,128)} fusion(bf16[8,128,256,1]{2,1,3,0:T(8,128)(2,1)S(1)} %bitcast.47, bf16[8,4,128,128]{3,2,1,0:T(8,128)(2,1)S(1)} %copy-done), kind=kOutput, calls=%fused_computation.1 | convolution fusion | flops 268435456 | bytes 5767168 | tf_op jit(solution)/shard_map/csij,cjf->csif/dot_general | solution.py:55
  62.5 5.5 %copy.31 = f32[8,4,128,256]{3,0,1,2:T(8,128)} copy(f32[8,4,128,256]{2,3,1,0:T(8,128)} %convolution_bitcast_fusion) | data formatting | bytes 8388608 | tf_op jit(solution)/shard_map/csij,cjf->csif/dot_general | solution.py:55
  68.0 4.0 %convolution_bitcast_fusion.1 = f32[4,128,256]{2,0,1:T(4,128)S(1)} fusion(f32[8,4,128,256]{3,0,1,2:T(8,128)} %copy.31, s32[8,4]{0,1:T(4,128)S(1)} %get-tuple-element.2, pred[8,4]{0,1:T(4,128)(4,1)S(1)} %get-tuple-element.4), kind=kOutput, calls=%fused_computation.8 | convolution fusion | flops 50331904 | bytes 4718752 | tf_op jit(solution)/shard_map/csh,csif->hif/dot_general | solution.py:56
  72.0 0.1 copy.32
  72.1 0.1 bitcast_multiply_fusion
  72.2 0.6 fusion.11
  72.9 0.3 all_to_all.17
  73.1 14.0 %all_to_all.21 = f32[32,1,2048]{2,1,0:T(1,128)S(1)} all-to-all(f32[32,1,2048]{2,1,0:T(1,128)S(1)} %all_to_all.17), channel_id=1, replica_groups=mesh['grp'=8,'rep'=4] {'grp','rep'}, dimensions={0} | all-to-all | bytes 524288 | tf_op jit(solution)/shard_map/all_to_all | solution.py:24
  87.2 0.2 reduce_sum.19
  87.3 0.1 broadcast_in_dim.48
  87.5 12.7 %all_to_all.22 = f32[32,1,2048]{2,1,0:T(1,128)S(1)} all-to-all(f32[32,1,2048]{2,1,0:T(1,128)S(1)} %broadcast_in_dim.48), channel_id=1, replica_groups=mesh['grp'=8,'rep'=4] {'grp','rep'}, dimensions={0} | all-to-all | bytes 524288 | tf_op jit(solution)/shard_map/all_to_all | solution.py:26
  100.2 0.6 reduce.2
  100.8 0.7 reshape.44
  (11 shorter events, 0.2 us)
Async XLA Ops:
  0.6 26.7 %copy-start = (bf16[8,4,128,128]{3,2,1,0:T(8,128)(2,1)S(1)}, bf16[8,4,128,128]{3,2,1,0:T(8,128)(2,1)}, u32[]{:S(2)}) copy-start(bf16[8,4,128,128]{3,2,1,0:T(8,128)(2,1)} %param.12) | copy-start | bytes 3145732
  4.2 9.8 %collective-permute-start = (bf16[128,640]{1,0:T(8,128)(2,1)S(1)}, bf16[128,640]{1,0:T(8,128)(2,1)S(1)}, u32[]{:S(2)}, u32[]{:S(2)}) collective-permute-start(bf16[128,640]{1,0:T(8,128)(2,1)S(1)} %pad_maximum_fusion), channel_id=1, source_target_pairs={{1,0},{2,1},{3,2},{0,3},{5,4},{6,5},{7,6},{4,7},{9,8},{10,9},{11,1... | collective-permute-start | bytes 491528 | tf_op jit(solution)/shard_map/ppermute | solution.py:14
  9.3 13.9 %collective-permute-start.1 = (bf16[128,640]{1,0:T(8,128)(2,1)S(1)}, bf16[128,640]{1,0:T(8,128)(2,1)S(1)}, u32[]{:S(2)}, u32[]{:S(2)}) collective-permute-start(bf16[128,640]{1,0:T(8,128)(2,1)S(1)} %pad_maximum_fusion), channel_id=1, source_target_pairs={{2,0},{3,1},{0,2},{1,3},{6,4},{7,5},{4,6},{5,7},{10,8},{11,9},{8,1... | collective-permute-start | bytes 491528 | tf_op jit(solution)/shard_map/ppermute | solution.py:14
  9.3 13.9 %collective-permute-start.2 = (bf16[128,640]{1,0:T(8,128)(2,1)S(1)}, bf16[128,640]{1,0:T(8,128)(2,1)S(1)}, u32[]{:S(2)}, u32[]{:S(2)}) collective-permute-start(bf16[128,640]{1,0:T(8,128)(2,1)S(1)} %pad_maximum_fusion), channel_id=1, source_target_pairs={{3,0},{0,1},{1,2},{2,3},{7,4},{4,5},{5,6},{6,7},{11,8},{8,9},{9,10... | collective-permute-start | bytes 491528 | tf_op jit(solution)/shard_map/ppermute | solution.py:14
  23.4 0.8 copy-start.1
  30.7 3.9 %copy-start.2 = (bf16[4,128,640]{2,1,0:T(8,128)(2,1)S(1)}, bf16[4,128,640]{2,1,0:T(8,128)(2,1)}, u32[]{:S(2)}) copy-start(bf16[4,128,640]{2,1,0:T(8,128)(2,1)} %copy-done.1) | copy-start | bytes 1966084
  30.7 19.3 %all-to-all-start = ((f32[8,128,256]{1,2,0:T(8,128)}), f32[8,128,256]{1,2,0:T(8,128)S(1)}, u32[]{:S(2)}, u32[]{:S(2)}) async-start(f32[8,128,256]{1,2,0:T(8,128)} %fusion.5), calls=%async_computation | async-start | bytes 2097152 | tf_op jit(solution)/shard_map/all_to_all | solution.py:68
  34.6 15.6 %copy-start.3 = (bf16[128,256]{1,0:T(8,128)(2,1)S(1)}, bf16[128,256]{1,0:T(8,128)(2,1)}, u32[]{:S(2)}) copy-start(bf16[128,256]{1,0:T(8,128)(2,1)} %param.7) | copy-start | bytes 196612
where the time goes:
time: 102 us
  blocking collectives  35.7 us (35%)
  waiting for transfers between devices  26.3 us (26%)
  matrix products  11.8 us (12%)
  local copies, waits for them, and re-layouts  11.4 us (11%)
  starting transfers between devices  9.98 us (10%)
  other arithmetic  5.58 us (5%)
    all_to_all x1, waiting for transfers between devices, per_device(): terms = lax.all_to_all(result, 'grp', 0, 0, tiled=True)  15.2 us
    all_to_all x1, blocking collectives, all_reduce_a2a(): lax.all_to_all(chunks, axes, 0, 0, tiled=True).reshape(count, -1).sum(0)  14 us
    all_to_all x1, blocking collectives, all_reduce_a2a(): return lax.all_to_all(spread, axes, 0, 0, tiled=True).reshape(w.shape)  12.7 us
    ppermute x3, waiting for transfers between devices, gather_rep(): lax.ppermute(x, 'rep', [((i + shift) % reps, i) for i in range(reps)])  11.1 us
    all_gather x1, blocking collectives, per_device(): lax.all_gather(scaled, 'grp', axis=0, tiled=True)  8.89 us
    ppermute x3, starting transfers between devices, gather_rep(): lax.ppermute(x, 'rep', [((i + shift) % reps, i) for i in range(reps)])  6.12 us
    dot_general x1, local copies, waits for them, and re-layouts, per_device(): jnp.einsum('csij,cjf->csif', tile_values, columns, preferred_element_type...  5.51 us
    dot_general x1, matrix products, per_device(): partial = jnp.einsum('csh,csif->hif', onehot, product, precision=HIGHEST)  4.02 us
  transfers between devices with their start and end apart: 4, of which 3 were waited for; matrix products, arithmetic and copies ran while one was open for 2% of the time, Pallas kernels for 0%

commit v1 on v0

--- a/solution.py
+++ b/solution.py
@@ -4,6 +4,18 @@
 from jax.sharding import PartitionSpec as P
 
 HIGHEST = lax.Precision.HIGHEST
+
+
+def collect(value, axis, dim):
+    ways, here, step = (lax.axis_size(axis), lax.axis_index(axis), value.shape[dim])
+    line, have = (value, 1)
+    while have < ways:
+        line = jnp.concatenate(
+            [line, lax.ppermute(line, axis, [(d, (d - have) % ways) for d in range(ways)])],
+            axis=dim,
+        )
+        have = 2 * have
+    return jnp.roll(line, here * step, axis=dim)
 
 
 def gather_rep(x):
@@ -40,7 +52,7 @@
         )
         * inverse
     ).astype(jnp.bfloat16)
-    columns = lax.all_gather(scaled, "grp", axis=0, tiled=True).reshape(col_tiles, edge, width)
+    columns = collect(scaled, "grp", 0).reshape(col_tiles, edge, width)
     degree_lanes = jnp.broadcast_to(degree.astype(jnp.bfloat16)[:, None], (rows_here, 128))
     packed = jnp.concatenate([projected, grad_pre, degree_lanes], axis=1)
     block = gather_rep(packed).reshape(reps * rows_here, -1)

time: 102 us -> 95 us (0.931)
  blocking collectives: 35.7 us -> 0 us
  waiting for transfers between devices: 26.3 us -> 40.9 us
  starting transfers between devices: 9.98 us -> 21.2 us
  other arithmetic: 5.58 us -> 7.48 us
    all_to_all x2 -> x0, blocking collectives: 26.8 us -> none  [the longest x1 14 us: all_reduce_a2a(): lax.all_to_all(chunks, axes, 0, 0, tiled=True).reshape(count, -1).sum(0)]
    all_to_all x0 -> x2, waiting for transfers between devices: none -> 12.7 us  [the longest x1 9.29 us: all_reduce_a2a(): return lax.all_to_all(spread, axes, 0, 0, tiled=True).reshape(w.shape)]
    all_gather x1 -> x0, blocking collectives: 8.89 us -> none  [per_device(): lax.all_gather(scaled, 'grp', axis=0, tiled=True)]
    all_to_all x0 -> x2, starting transfers between devices: none -> 7.38 us  [the longest x1 4.8 us: all_reduce_a2a(): lax.all_to_all(chunks, axes, 0, 0, tiled=True).reshape(count, -1).sum(0)]
    ppermute x0 -> x3, waiting for transfers between devices: none -> 6.54 us  [collect(): lax.ppermute(line, axis, [(d, (d - have) % ways) for d in range(ways)])]
    ppermute x0 -> x3, starting transfers between devices: none -> 4.14 us  [collect(): lax.ppermute(line, axis, [(d, (d - have) % ways) for d in range(ways)])]
    ppermute x3, waiting for transfers between devices: 11.1 us -> 7.43 us  [gather_rep(): lax.ppermute(x, 'rep', [((i + shift) % reps, i) for i in range(reps)])]
  transfers between devices with their start and end apart: 4 -> 9, of which waited for: 3 -> 6; matrix products, arithmetic and copies ran while one was open for 2% -> 12% of each run, Pallas kernels for 0% -> 0%
where the time goes in v1:
time: 95 us; the launch traced here: 94.3 us
  waiting for transfers between devices  40.9 us (43%)
  starting transfers between devices  21.2 us (22%)
  local copies, waits for them, and re-layouts  12.1 us (13%)
  matrix products  11.8 us (12%)
  other arithmetic  7.48 us (8%)
    all_to_all x1, waiting for transfers between devices, per_device(): terms = lax.all_to_all(result, 'grp', 0, 0, tiled=True)  14.2 us
    all_to_all x1, waiting for transfers between devices, all_reduce_a2a(): return lax.all_to_all(spread, axes, 0, 0, tiled=True).reshape(w.shape)  9.29 us
    ppermute x3, waiting for transfers between devices, gather_rep(): lax.ppermute(x, 'rep', [((i + shift) % reps, i) for i in range(reps)])  7.43 us
    ppermute x3, waiting for transfers between devices, collect(): lax.ppermute(line, axis, [(d, (d - have) % ways) for d in range(ways)])  6.54 us
    ppermute x3, starting transfers between devices, gather_rep(): lax.ppermute(x, 'rep', [((i + shift) % reps, i) for i in range(reps)])  6.12 us
    dot_general x1, local copies, waits for them, and re-layouts, per_device(): jnp.einsum('csij,cjf->csif', tile_values, columns, preferred_element_type...  5.5 us
    all_to_all x1, starting transfers between devices, all_reduce_a2a(): lax.all_to_all(chunks, axes, 0, 0, tiled=True).reshape(count, -1).sum(0)  4.8 us
    ppermute x3, starting transfers between devices, collect(): lax.ppermute(line, axis, [(d, (d - have) % ways) for d in range(ways)])  4.14 us
  transfers between devices with their start and end apart: 9, of which 6 were waited for; matrix products, arithmetic and copies ran while one was open for 12% of the time, Pallas kernels for 0%

profile of v1, /device:TPU:0, one launch (start us, length us, event | category | flops | bytes accessed | tf_op | source)
XLA Modules:
  0.0 94.3 jit_solution(4907564032630039334)
XLA Ops:
  0.6 0.0 copy-start
  0.6 0.7 convert_rsqrt_fusion
  1.4 0.7 convert_element_type.22
  2.1 0.9 compare_select_fusion
  2.9 1.1 %fusion.8 = bf16[128,256]{1,0:T(8,128)(2,1)S(1)} fusion(bf16[128,256]{1,0:T(8,128)(2,1)S(1)} %compare_select_fusion, bf16[256,256]{1,0:T(8,128)(2,1)} %param.8, f32[128]{0:T(128)S(1)} %convert_rsqrt_fusion), kind=kOutput, calls=%fused_computation.10 | convolution fusion | flops 16842752 | bytes 262656 | tf_op jit(solution)/shard_map/dot_general | solution.py:50
  4.0 0.1 broadcast_in_dim.44
  4.2 5.1 %collective-permute-start = (bf16[128,640]{1,0:T(8,128)(2,1)S(1)}, bf16[128,640]{1,0:T(8,128)(2,1)S(1)}, u32[]{:S(2)}, u32[]{:S(2)}) collective-permute-start(bf16[128,640]{1,0:T(8,128)(2,1)S(1)} %pad_maximum_fusion.1), channel_id=1, source_target_pairs={{1,0},{2,1},{3,2},{0,3},{5,4},{6,5},{7,6},{4,7},{9,8},{10,9},{11,1... | collective-permute-start | bytes 491528 | tf_op jit(solution)/shard_map/ppermute | solution.py:26
  9.3 0.0 collective-permute-start.1
  9.3 1.0 %collective-permute-start.2 = (bf16[128,640]{1,0:T(8,128)(2,1)S(1)}, bf16[128,640]{1,0:T(8,128)(2,1)S(1)}, u32[]{:S(2)}, u32[]{:S(2)}) collective-permute-start(bf16[128,640]{1,0:T(8,128)(2,1)S(1)} %pad_maximum_fusion.1), channel_id=1, source_target_pairs={{3,0},{0,1},{1,2},{2,3},{7,4},{4,5},{5,6},{6,7},{11,8},{8,9},{9,10... | collective-permute-start | bytes 491528 | tf_op jit(solution)/shard_map/ppermute | solution.py:26
  10.3 0.9 constant_dynamic-update-slice_fusion.7
  11.2 1.1 %collective-permute-start.3 = (bf16[128,256]{1,0:T(8,128)(2,1)S(1)}, bf16[128,256]{1,0:T(8,128)(2,1)S(1)}, u32[]{:S(2)}, u32[]{:S(2)}) collective-permute-start(bf16[128,256]{1,0:T(8,128)(2,1)S(1)} %get-tuple-element.3), channel_id=1, source_target_pairs={{0,28},{4,0},{8,4},{12,8},{16,12},{20,16},{24,20},{28,24},{1,29},{... | collective-permute-start | bytes 196616 | tf_op jit(solution)/shard_map/ppermute | solution.py:14
  12.3 0.7 broadcast_compare_fusion
  13.0 0.7 broadcast_select_fusion
  13.7 0.5 collective-permute-done.3
  14.2 1.5 %collective-permute-start.4 = (bf16[256,256]{1,0:T(8,128)(2,1)S(1)}, bf16[256,256]{1,0:T(8,128)(2,1)S(1)}, u32[]{:S(2)}, u32[]{:S(2)}) collective-permute-start(bf16[256,256]{1,0:T(8,128)(2,1)S(1)} %pad_maximum_fusion.2), channel_id=1, source_target_pairs={{0,24},{4,28},{8,0},{12,4},{16,8},{20,12},{24,16},{28,20},{1,25},{... | collective-permute-start | bytes 393224 | tf_op jit(solution)/shard_map/ppermute | solution.py:14
  15.7 0.0 collective-permute-done
  15.7 7.4 %collective-permute-done.1 = bf16[128,640]{1,0:T(8,128)(2,1)S(1)} collective-permute-done((bf16[128,640]{1,0:T(8,128)(2,1)S(1)}, bf16[128,640]{1,0:T(8,128)(2,1)S(1)}, u32[]{:S(2)}, u32[]{:S(2)}) %collective-permute-start.1) | collective-permute-done | bytes 163872 | tf_op jit(solution)/shard_map/ppermute | solution.py:26
  23.2 0.0 collective-permute-done.2
  23.3 0.0 collective-permute-done.4
  23.4 1.6 %collective-permute-start.5 = (bf16[512,256]{1,0:T(8,128)(2,1)S(1)}, bf16[512,256]{1,0:T(8,128)(2,1)S(1)}, u32[]{:S(2)}, u32[]{:S(2)}) collective-permute-start(bf16[512,256]{1,0:T(8,128)(2,1)S(1)} %pad_maximum_fusion), channel_id=1, source_target_pairs={{0,16},{4,20},{8,24},{12,28},{16,0},{20,4},{24,8},{28,12},{1,17},{... | collective-permute-start | bytes 786440 | tf_op jit(solution)/shard_map/ppermute | solution.py:14
  25.0 0.1 constant_dynamic-slice_fusion.1
  25.0 0.2 rsqrt_reduce_fusion
  25.2 6.0 %collective-permute-done.5 = bf16[512,256]{1,0:T(8,128)(2,1)S(1)} collective-permute-done((bf16[512,256]{1,0:T(8,128)(2,1)S(1)}, bf16[512,256]{1,0:T(8,128)(2,1)S(1)}, u32[]{:S(2)}, u32[]{:S(2)}) %collective-permute-start.5) | collective-permute-done | bytes 262176 | tf_op jit(solution)/shard_map/ppermute | solution.py:14
  31.4 0.0 copy-done
  31.4 2.7 %convolution_bitcast_fusion = f32[8,4,128,256]{2,3,1,0:T(8,128)} fusion(bf16[8,128,256,1]{2,1,3,0:T(8,128)(2,1)S(1)} %bitcast.47, bf16[8,4,128,128]{3,2,1,0:T(8,128)(2,1)S(1)} %copy-done), kind=kOutput, calls=%fused_computation.1 | convolution fusion | flops 268435456 | bytes 5767168 | tf_op jit(solution)/shard_map/csij,cjf->csif/dot_general | solution.py:67
  34.1 5.5 %copy.37 = f32[8,4,128,256]{3,0,1,2:T(8,128)} copy(f32[8,4,128,256]{2,3,1,0:T(8,128)} %convolution_bitcast_fusion) | data formatting | bytes 8388608 | tf_op jit(solution)/shard_map/csij,cjf->csif/dot_general | solution.py:67
  39.6 4.0 %convolution_bitcast_fusion.1 = f32[4,128,256]{2,0,1:T(4,128)S(1)} fusion(f32[8,4,128,256]{3,0,1,2:T(8,128)} %copy.37, s32[8,4]{0,1:T(4,128)S(1)} %get-tuple-element.4, pred[8,4]{0,1:T(4,128)(4,1)S(1)} %get-tuple-element.6), kind=kOutput, calls=%fused_computation.8 | convolution fusion | flops 50331904 | bytes 4718752 | tf_op jit(solution)/shard_map/csh,csif->hif/dot_general | solution.py:68
  43.6 0.1 copy.38
  43.7 0.1 bitcast_multiply_fusion
  43.9 0.6 fusion.11
  44.5 1.0 %all_to_all.17 = f32[32,1,2048]{2,1,0:T(1,128)} reshape(f32[256,256]{1,0:T(8,128)S(1)} %fusion.11) | data formatting | bytes 524288 | tf_op jit(solution)/shard_map/all_to_all | solution.py:36
  45.4 4.8 %all-to-all-start.1 = ((f32[32,1,2048]{2,1,0:T(1,128)}), f32[32,1,2048]{2,1,0:T(1,128)}, u32[]{:S(2)}, u32[]{:S(2)}) async-start(f32[32,1,2048]{2,1,0:T(1,128)} %all_to_all.17), calls=%async_computation.1 | async-start | bytes 524288 | tf_op jit(solution)/shard_map/all_to_all | solution.py:36
  50.2 0.1 copy.31
  50.3 0.1 copy.33
  50.4 0.1 reshape.47
  50.5 0.1 copy.32
  50.6 0.7 gather_fusion
  51.3 2.4 %copy.34 = bf16[8,4,128,256]{2,3,1,0:T(8,128)(2,1)} copy(bf16[8,4,128,256]{3,2,1,0:T(8,128)(2,1)S(1)} %bitcast.43) | data formatting | bytes 4194304 | tf_op jit(solution)/shard_map/jit(_take)/gather | solution.py:77
  53.7 3.3 %fusion.5 = f32[8,128,256]{1,2,0:T(8,128)} fusion(bf16[8,4,128,128]{3,2,1,0:T(8,128)(2,1)S(1)} %copy-done, bf16[8,4,128,256]{2,3,1,0:T(8,128)(2,1)} %copy.34, pred[8,4]{1,0:T(8,128)(4,1)S(1)} %copy.32, pred[8,4]{1,0:T(8,128)(4,1)S(1)} %copy.31), kind=kOutput, calls=%fused_computation.7 | convolution fusion | flops 270532608 | bytes 4194368 | tf_op jit(solution)/shard_map/csij,csif->cjf/dot_general | solution.py:79
  57.0 3.4 %all-to-all-done.1 = f32[32,1,2048]{2,1,0:T(1,128)} async-done(((f32[32,1,2048]{2,1,0:T(1,128)}), f32[32,1,2048]{2,1,0:T(1,128)}, u32[]{:S(2)}, u32[]{:S(2)}) %all-to-all-start.1) | async-done | bytes 262176 | tf_op jit(solution)/shard_map/all_to_all | solution.py:36
  60.4 3.6 %all-to-all-start = ((f32[8,128,256]{1,2,0:T(8,128)}), f32[8,128,256]{1,2,0:T(8,128)S(1)}, u32[]{:S(2)}, u32[]{:S(2)}) async-start(f32[8,128,256]{1,2,0:T(8,128)} %fusion.5), calls=%async_computation | async-start | bytes 2097152 | tf_op jit(solution)/shard_map/all_to_all | solution.py:80
  64.0 1.1 %reduce_sum.19 = f32[2048]{0:T(1024)S(1)} reduce(f32[32,1,2048]{2,1,0:T(1,128)} %all-to-all-done.1, f32[]{:T(128)} %constant.65.clone.1), dimensions={0,1}, to_apply=%region_1.2 | reduce | flops 63488 | bytes 270340 | tf_op jit(solution)/shard_map/reduce_sum | solution.py:36
  65.1 14.2 %all-to-all-done = f32[8,128,256]{1,2,0:T(8,128)S(1)} async-done(((f32[8,128,256]{1,2,0:T(8,128)}), f32[8,128,256]{1,2,0:T(8,128)S(1)}, u32[]{:S(2)}, u32[]{:S(2)}) %all-to-all-start) | async-done | bytes 1048608 | tf_op jit(solution)/shard_map/all_to_all | solution.py:80
  79.3 0.8 broadcast_in_dim.48
  80.2 2.6 %all-to-all-start.2 = ((f32[32,1,2048]{2,1,0:T(1,128)}), f32[32,1,2048]{2,1,0:T(1,128)S(1)}, u32[]{:S(2)}, u32[]{:S(2)}) async-start(f32[32,1,2048]{2,1,0:T(1,128)} %broadcast_in_dim.48), calls=%async_computation.2 | async-start | bytes 524288 | tf_op jit(solution)/shard_map/all_to_all | solution.py:38
  82.8 0.1 reduce_sum.18
  82.8 0.1 copy.35
  82.9 0.7 broadcast_multiply_fusion
  83.7 9.3 %all-to-all-done.2 = f32[32,1,2048]{2,1,0:T(1,128)S(1)} async-done(((f32[32,1,2048]{2,1,0:T(1,128)}), f32[32,1,2048]{2,1,0:T(1,128)S(1)}, u32[]{:S(2)}, u32[]{:S(2)}) %all-to-all-start.2) | async-done | bytes 262176 | tf_op jit(solution)/shard_map/all_to_all | solution.py:38
  93.0 0.6 reduce.2
  93.6 0.7 reshape.44
  (21 shorter events, 0.4 us)
Async XLA Ops:
  0.6 30.7 %copy-start = (bf16[8,4,128,128]{3,2,1,0:T(8,128)(2,1)S(1)}, bf16[8,4,128,128]{3,2,1,0:T(8,128)(2,1)}, u32[]{:S(2)}) copy-start(bf16[8,4,128,128]{3,2,1,0:T(8,128)(2,1)} %param.12) | copy-start | bytes 3145732
  4.2 11.5 %collective-permute-start = (bf16[128,640]{1,0:T(8,128)(2,1)S(1)}, bf16[128,640]{1,0:T(8,128)(2,1)S(1)}, u32[]{:S(2)}, u32[]{:S(2)}) collective-permute-start(bf16[128,640]{1,0:T(8,128)(2,1)S(1)} %pad_maximum_fusion.1), channel_id=1, source_target_pairs={{1,0},{2,1},{3,2},{0,3},{5,4},{6,5},{7,6},{4,7},{9,8},{10,9},{11,1... | collective-permute-start | bytes 491528 | tf_op jit(solution)/shard_map/ppermute | solution.py:26
  9.3 13.9 %collective-permute-start.1 = (bf16[128,640]{1,0:T(8,128)(2,1)S(1)}, bf16[128,640]{1,0:T(8,128)(2,1)S(1)}, u32[]{:S(2)}, u32[]{:S(2)}) collective-permute-start(bf16[128,640]{1,0:T(8,128)(2,1)S(1)} %pad_maximum_fusion.1), channel_id=1, source_target_pairs={{2,0},{3,1},{0,2},{1,3},{6,4},{7,5},{4,6},{5,7},{10,8},{11,9},{8,1... | collective-permute-start | bytes 491528 | tf_op jit(solution)/shard_map/ppermute | solution.py:26
  9.3 13.9 %collective-permute-start.2 = (bf16[128,640]{1,0:T(8,128)(2,1)S(1)}, bf16[128,640]{1,0:T(8,128)(2,1)S(1)}, u32[]{:S(2)}, u32[]{:S(2)}) collective-permute-start(bf16[128,640]{1,0:T(8,128)(2,1)S(1)} %pad_maximum_fusion.1), channel_id=1, source_target_pairs={{3,0},{0,1},{1,2},{2,3},{7,4},{4,5},{5,6},{6,7},{11,8},{8,9},{9,10... | collective-permute-start | bytes 491528 | tf_op jit(solution)/shard_map/ppermute | solution.py:26
  11.2 3.0 %collective-permute-start.3 = (bf16[128,256]{1,0:T(8,128)(2,1)S(1)}, bf16[128,256]{1,0:T(8,128)(2,1)S(1)}, u32[]{:S(2)}, u32[]{:S(2)}) collective-permute-start(bf16[128,256]{1,0:T(8,128)(2,1)S(1)} %get-tuple-element.3), channel_id=1, source_target_pairs={{0,28},{4,0},{8,4},{12,8},{16,12},{20,16},{24,20},{28,24},{1,29},{... | collective-permute-start | bytes 196616 | tf_op jit(solution)/shard_map/ppermute | solution.py:14
  14.2 9.1 %collective-permute-start.4 = (bf16[256,256]{1,0:T(8,128)(2,1)S(1)}, bf16[256,256]{1,0:T(8,128)(2,1)S(1)}, u32[]{:S(2)}, u32[]{:S(2)}) collective-permute-start(bf16[256,256]{1,0:T(8,128)(2,1)S(1)} %pad_maximum_fusion.2), channel_id=1, source_target_pairs={{0,24},{4,28},{8,0},{12,4},{16,8},{20,12},{24,16},{28,20},{1,25},{... | collective-permute-start | bytes 393224 | tf_op jit(solution)/shard_map/ppermute | solution.py:14
  23.4 7.8 %collective-permute-start.5 = (bf16[512,256]{1,0:T(8,128)(2,1)S(1)}, bf16[512,256]{1,0:T(8,128)(2,1)S(1)}, u32[]{:S(2)}, u32[]{:S(2)}) collective-permute-start(bf16[512,256]{1,0:T(8,128)(2,1)S(1)} %pad_maximum_fusion), channel_id=1, source_target_pairs={{0,16},{4,20},{8,24},{12,28},{16,0},{20,4},{24,8},{28,12},{1,17},{... | collective-permute-start | bytes 786440 | tf_op jit(solution)/shard_map/ppermute | solution.py:14
  45.4 15.0 %all-to-all-start.1 = ((f32[32,1,2048]{2,1,0:T(1,128)}), f32[32,1,2048]{2,1,0:T(1,128)}, u32[]{:S(2)}, u32[]{:S(2)}) async-start(f32[32,1,2048]{2,1,0:T(1,128)} %all_to_all.17), calls=%async_computation.1 | async-start | bytes 524288 | tf_op jit(solution)/shard_map/all_to_all | solution.py:36
  60.4 18.9 %all-to-all-start = ((f32[8,128,256]{1,2,0:T(8,128)}), f32[8,128,256]{1,2,0:T(8,128)S(1)}, u32[]{:S(2)}, u32[]{:S(2)}) async-start(f32[8,128,256]{1,2,0:T(8,128)} %fusion.5), calls=%async_computation | async-start | bytes 2097152 | tf_op jit(solution)/shard_map/all_to_all | solution.py:80
  80.2 12.8 %all-to-all-start.2 = ((f32[32,1,2048]{2,1,0:T(1,128)}), f32[32,1,2048]{2,1,0:T(1,128)S(1)}, u32[]{:S(2)}, u32[]{:S(2)}) async-start(f32[32,1,2048]{2,1,0:T(1,128)} %broadcast_in_dim.48), calls=%async_computation.2 | async-start | bytes 524288 | tf_op jit(solution)/shard_map/all_to_all | solution.py:38
